TPU v7x, 512 devices: a whole 4x8x8 slice. The times are simulated.
512 devices in a mesh: dp: 32 (over x, y), expert: 16 (over z, core).
Axes of the slice: x: 4, y: 8, z: 8, core: 2. Of those that a mesh axis runs over, the one named last changes fastest.
Arguments:
- tokens: bfloat16 [65536, 2048], P(('dp', 'expert')), may hold values from -6 to 6
- cotangent: bfloat16 [65536, 2048], P(('dp', 'expert')), may hold values from -6 to 6
- expert_ids: int32 [65536, 2], P(('dp', 'expert')), may hold values from 0 to 15, as said below
- router_probs: float32 [65536, 2], P(('dp', 'expert')), may hold values from 0.1 to 1
- gate_weight: bfloat16 [16, 2048, 768], P('expert', 'dp'), may hold values from -0.125 to 0.125
- up_weight: bfloat16 [16, 2048, 768], P('expert', 'dp'), may hold values from -0.125 to 0.125
- down_weight: bfloat16 [16, 768, 2048], P('expert', 'dp'), may hold values from -0.21875 to 0.21875
Outputs:
- mixed_out: bfloat16 [65536, 2048], P(('dp', 'expert'))
- grad_tokens: bfloat16 [65536, 2048], P(('dp', 'expert'))
- grad_probs: float32 [65536, 2], P(('dp', 'expert'))
- grad_down: bfloat16 [16, 768, 2048], P('expert', 'dp')
Inputs may be any that keep to these rules, and one draw needn't show every extreme that they name: `expert_ids`: each token names 2 different experts. In each aligned block of 128 tokens (the tokens of one device) no expert is named more than 18 times, and in each aligned group of 16 such blocks one expert is named exactly 18 times in every block of the group.
All inputs are finite; a program needn't handle non-finite values.
Results may differ from a plain program's by a relative error of at most 0.023.
Values may be sent and summed in bfloat16 or wider, within the bound.
No kernel may reach another device: no remote copies, remote signals or barrier semaphores. Data moves between devices by JAX's collectives and lax.ppermute only.
A program may use at most 64 MiB of HBM per device.

v0:
```python
import jax
import jax.numpy as jnp
from jax import lax
from jax.sharding import PartitionSpec as P


def shards(tokens, cotangent, expert_ids, router_probs, gate_weight, up_weight, down_weight):
    tok_count = tokens.shape[0]
    features = tokens.shape[1]
    choices_each = expert_ids.shape[1]
    slot_total = tok_count * choices_each
    groups = lax.axis_size("expert")
    capacity = 9 * slot_total // (8 * groups)
    slot_count = groups * capacity
    flat_ids = expert_ids.reshape(slot_total)
    member = (flat_ids[:, None] == jnp.arange(groups, dtype=jnp.int32)[None, :]).astype(jnp.int32)
    before = jnp.cumsum(member, axis=0) - member
    target = flat_ids * capacity + jnp.sum(before * member, axis=1)
    placer = (target[None, :] == jnp.arange(slot_count, dtype=jnp.int32)[:, None]).astype(
        jnp.bfloat16
    )
    placer_tok = jnp.sum(placer.reshape(slot_count, tok_count, choices_each), axis=2)
    weighted = (
        (router_probs[:, :, None] * cotangent.astype(jnp.float32)[:, None, :])
        .astype(jnp.bfloat16)
        .reshape(slot_total, features)
    )
    send_rows = jnp.dot(placer_tok, tokens, preferred_element_type=jnp.float32).astype(jnp.bfloat16)
    send_grad = jnp.dot(placer, weighted, preferred_element_type=jnp.float32).astype(jnp.bfloat16)
    recv_rows, recv_grad = (
        lax.all_to_all(
            send_rows.reshape(groups, capacity, features),
            "expert",
            split_axis=0,
            concat_axis=0,
            tiled=True,
        ),
        lax.all_to_all(
            send_grad.reshape(groups, capacity, features),
            "expert",
            split_axis=0,
            concat_axis=0,
            tiled=True,
        ),
    )
    x_rows = recv_rows.reshape(slot_count, features)
    dy_rows = recv_grad.reshape(slot_count, features)
    w_gate, w_up = (
        lax.all_gather(gate_weight[0], "dp", axis=0, tiled=True),
        lax.all_gather(up_weight[0], "dp", axis=0, tiled=True),
    )
    gate_pre = jnp.dot(x_rows, w_gate, preferred_element_type=jnp.float32)
    up_pre = jnp.dot(x_rows, w_up, preferred_element_type=jnp.float32)
    sig_gate = jax.nn.sigmoid(gate_pre)
    active = gate_pre * sig_gate
    hidden = (active * up_pre).astype(jnp.bfloat16)
    contract = (((1,), (1,)), ((), ()))
    weight_rows = lax.all_gather(down_weight[0], "dp", axis=0, tiled=True)
    part_hidden = hidden
    acc_part = jnp.dot(part_hidden, weight_rows, preferred_element_type=jnp.float32)
    back_part = lax.dot_general(dy_rows, weight_rows, contract, preferred_element_type=jnp.float32)
    output = acc_part.astype(jnp.bfloat16)
    grad_gate = (back_part * up_pre * sig_gate * (1.0 + gate_pre * (1.0 - sig_gate))).astype(
        jnp.bfloat16
    )
    grad_up = (back_part * active).astype(jnp.bfloat16)
    grad_rows = (
        lax.dot_general(grad_gate, w_gate, contract, preferred_element_type=jnp.float32)
        + lax.dot_general(grad_up, w_up, contract, preferred_element_type=jnp.float32)
    ).astype(jnp.bfloat16)
    back_out, back_grad = (
        lax.all_to_all(
            output.reshape(groups, capacity, features),
            "expert",
            split_axis=0,
            concat_axis=0,
            tiled=True,
        ),
        lax.all_to_all(
            grad_rows.reshape(groups, capacity, features),
            "expert",
            split_axis=0,
            concat_axis=0,
            tiled=True,
        ),
    )
    unplace = (((0,), (0,)), ((), ()))
    gathered = lax.dot_general(
        placer, back_out.reshape(slot_count, features), unplace, preferred_element_type=jnp.float32
    )
    gathered = gathered.reshape(tok_count, choices_each, features)
    grad_tokens = lax.dot_general(
        placer_tok,
        back_grad.reshape(slot_count, features),
        unplace,
        preferred_element_type=jnp.float32,
    ).astype(jnp.bfloat16)
    mixed_out = jnp.sum(router_probs[:, :, None] * gathered, axis=1).astype(jnp.bfloat16)
    grad_probs = jnp.sum(cotangent.astype(jnp.float32)[:, None, :] * gathered, axis=2)
    part_hidden = hidden
    grad_down = lax.psum_scatter(
        lax.dot_general(
            part_hidden, dy_rows, (((0,), (0,)), ((), ())), preferred_element_type=jnp.float32
        ).astype(jnp.bfloat16),
        "dp",
        scatter_dimension=0,
        tiled=True,
    )[None]
    return (mixed_out, grad_tokens, grad_probs, grad_down)


def solution(mesh):
    placed = (
        P(("dp", "expert"), None),
        P(("dp", "expert"), None),
        P(("dp", "expert"), None),
        P(("dp", "expert"), None),
        P("expert", "dp", None),
        P("expert", "dp", None),
        P("expert", "dp", None),
    )
    return jax.shard_map(
        shards,
        mesh=mesh,
        in_specs=placed,
        out_specs=(
            P(("dp", "expert"), None),
            P(("dp", "expert"), None),
            P(("dp", "expert"), None),
            P("expert", "dp", None),
        ),
        check_vma=False,
    )
```

profile of v0, /device:TPU:16, one launch (start us, length us, event | category | flops | bytes accessed | tf_op | source)
XLA Modules:
  0.0 505.6 jit_solution(4395308883108628984)
XLA Ops:
  7.2 0.7 all-gather.7.cloned.1.call-update
  8.0 0.7 all-gather.9.cloned.1.call-update
  8.7 0.7 all-gather.11.cloned.1.call-update
  9.4 0.8 copy.29
  10.2 0.1 reshape.94
  10.3 0.1 eq.65
  10.5 0.6 reduce-window.6
  11.1 0.2 slice_reduce_fusion
  11.4 0.1 reduce_sum.42
  11.6 0.7 multiply_add_fusion.1
  12.4 0.5 convolution_convert_fusion.1
  12.8 1.3 reshape.96
  14.2 10.6 %all-to-all-start = ((bf16[16,18,2048]{2,1,0:T(8,128)(2,1)}), bf16[16,18,2048]{2,1,0:T(8,128)(2,1)}, u32[]{:S(2)}, u32[]{:S(2)}) async-start(bf16[16,18,2048]{2,1,0:T(8,128)(2,1)} %reshape.96), calls=%async_computation | async-start | bytes 3145728 | tf_op jit(solution)/shard_map/all_to_all | solution.py:31
  24.8 0.1 copy.33
  24.9 0.1 mul.81
  25.0 1.0 mul.83.clone
  26.1 2.5 mul.84
  28.6 2.1 convolution_convert_fusion.2
  30.7 1.4 reshape.100
  32.1 30.6 %all-to-all-done = bf16[16,18,2048]{2,1,0:T(8,128)(2,1)} async-done(((bf16[16,18,2048]{2,1,0:T(8,128)(2,1)}), bf16[16,18,2048]{2,1,0:T(8,128)(2,1)}, u32[]{:S(2)}, u32[]{:S(2)}) %all-to-all-start) | async-done | bytes 1179680 | tf_op jit(solution)/shard_map/all_to_all | solution.py:31
  62.7 4.8 all-to-all-start.2
  67.5 2.4 reshape.97
  70.0 35.4 %all-to-all-done.2 = bf16[16,18,2048]{2,1,0:T(8,128)(2,1)S(1)} async-done(((bf16[16,18,2048]{2,1,0:T(8,128)(2,1)}), bf16[16,18,2048]{2,1,0:T(8,128)(2,1)S(1)}, u32[]{:S(2)}, u32[]{:S(2)}) %all-to-all-start.2) | async-done | bytes 1179680 | tf_op jit(solution)/shard_map/all_to_all | solution.py:38
  105.3 1.2 reshape.101
  106.6 4.3 fusion.10
  110.9 73.5 %all-gather.9.cloned.1.call-done = bf16[1,2048,768]{2,1,0:T(8,128)(2,1)} async-done(((bf16[1,64,768]{2,1,0:T(8,128)(2,1)}), bf16[1,2048,768]{2,1,0:T(8,128)(2,1)}) %all-gather.9.cloned.1.call-update) | async-done | bytes 3145744 | tf_op jit(solution)/shard_map/all_gather | solution.py:50
  184.4 4.1 multiply_convert_fusion.4
  188.5 0.8 copy-done.10
  189.3 3.6 convolution_convert_fusion
  192.9 76.5 %all-gather.11.cloned.1.call-done = bf16[1,768,2048]{2,1,0:T(8,128)(2,1)} async-done(((bf16[1,24,2048]{2,1,0:T(8,128)(2,1)}), bf16[1,768,2048]{2,1,0:T(8,128)(2,1)}) %all-gather.11.cloned.1.call-update) | async-done | bytes 3145744 | tf_op jit(solution)/shard_map/all_gather | solution.py:58
  269.4 3.0 fusion.18
  272.4 1.4 reshape.98
  273.7 7.5 %all-to-all-start.1 = ((bf16[16,18,2048]{2,1,0:T(8,128)(2,1)}), bf16[16,18,2048]{2,1,0:T(8,128)(2,1)S(1)}, u32[]{:S(2)}, u32[]{:S(2)}) async-start(bf16[16,18,2048]{2,1,0:T(8,128)(2,1)} %reshape.98), calls=%async_computation.1 | async-start | bytes 3145728 | tf_op jit(solution)/shard_map/all_to_all | solution.py:72
  281.2 3.5 fusion
  284.8 1.1 fusion.4
  285.9 0.7 copy-done.6
  286.7 0.2 copy-done.9
  286.9 2.2 fusion.15
  289.1 2.4 reshape.102
  291.5 27.6 %all-to-all-done.1 = bf16[16,18,2048]{2,1,0:T(8,128)(2,1)S(1)} async-done(((bf16[16,18,2048]{2,1,0:T(8,128)(2,1)}), bf16[16,18,2048]{2,1,0:T(8,128)(2,1)S(1)}, u32[]{:S(2)}, u32[]{:S(2)}) %all-to-all-start.1) | async-done | bytes 1179680 | tf_op jit(solution)/shard_map/all_to_all | solution.py:72
  319.1 4.8 all-to-all-start.3
  323.9 1.1 convert_element_type.58
  325.0 1.2 reshape.107
  326.2 35.6 %all-to-all-done.3 = bf16[16,18,2048]{2,1,0:T(8,128)(2,1)} async-done(((bf16[16,18,2048]{2,1,0:T(8,128)(2,1)}), bf16[16,18,2048]{2,1,0:T(8,128)(2,1)}, u32[]{:S(2)}, u32[]{:S(2)}) %all-to-all-start.3) | async-done | bytes 1179680 | tf_op jit(solution)/shard_map/all_to_all | solution.py:79
  361.8 1.6 reshape.103
  363.4 3.0 multiply_reduce_fusion
  366.5 1.3 convolution_convert_fusion.3
  367.7 131.4 %reduce-scatter.2.cloned.1.call-done = bf16[24,2048]{1,0:T(8,128)(2,1)} async-done(((bf16[768,2048]{1,0:T(8,128)(2,1)}), bf16[24,2048]{1,0:T(8,128)(2,1)}) %reduce-scatter.2.cloned.1.call-update) | async-done | bytes 98320 | tf_op jit(solution)/shard_map/reduce_scatter | solution.py:101
  (34 shorter events, 0.5 us)
Async XLA Ops:
  7.2 5.2 %copy-start = (bf16[128,2048]{1,0:T(8,128)(2,1)S(1)}, bf16[128,2048]{1,0:T(8,128)(2,1)}, u32[]{:S(2)}) copy-start(bf16[128,2048]{1,0:T(8,128)(2,1)} %param.7) | copy-start | bytes 1572868
  7.2 99.4 %all-gather.7.cloned.1.call-start = ((), (), s32[]{:S(2)}) async-start(), calls=%async_computation.6 | async-start | bytes 3244032 | tf_op jit(solution)/shard_map/all_gather | solution.py:49
  7.9 176.5 %all-gather.9.cloned.1.call-start = ((), (), s32[]{:S(2)}) async-start(), calls=%async_computation.7 | async-start | bytes 3244032 | tf_op jit(solution)/shard_map/all_gather | solution.py:50
  8.7 260.7 %all-gather.11.cloned.1.call-start = ((), (), s32[]{:S(2)}) async-start(), calls=%async_computation.8 | async-start | bytes 3244032 | tf_op jit(solution)/shard_map/all_gather | solution.py:58
  14.2 10.6 %copy-start.5 = (f32[128,2]{0,1:T(2,128)S(1)}, f32[128,2]{0,1:T(2,128)}, u32[]{:S(2)}) copy-start(f32[128,2]{0,1:T(2,128)} %param.10) | copy-start | bytes 3076
  14.2 10.9 %copy-start.1 = (bf16[128,2048]{1,0:T(8,128)(2,1)S(1)}, bf16[128,2048]{1,0:T(8,128)(2,1)}, u32[]{:S(2)}) copy-start(bf16[128,2048]{1,0:T(8,128)(2,1)} %param.8) | copy-start | bytes 1572868
  14.2 48.5 %all-to-all-start = ((bf16[16,18,2048]{2,1,0:T(8,128)(2,1)}), bf16[16,18,2048]{2,1,0:T(8,128)(2,1)}, u32[]{:S(2)}, u32[]{:S(2)}) async-start(bf16[16,18,2048]{2,1,0:T(8,128)(2,1)} %reshape.96), calls=%async_computation | async-start | bytes 3145728 | tf_op jit(solution)/shard_map/all_to_all | solution.py:31
  62.7 42.7 %all-to-all-start.2 = ((bf16[16,18,2048]{2,1,0:T(8,128)(2,1)}), bf16[16,18,2048]{2,1,0:T(8,128)(2,1)S(1)}, u32[]{:S(2)}, u32[]{:S(2)}) async-start(bf16[16,18,2048]{2,1,0:T(8,128)(2,1)} %reshape.100), calls=%async_computation.2 | async-start | bytes 3145728 | tf_op jit(solution)/shard_map/all_to_all | solution.py:38
  67.5 431.6 %reduce-scatter.2.cloned.1.call-start = ((), (), s32[]{:S(2)}) async-start(), calls=%async_computation.5 | async-start | bytes 3244032 | tf_op jit(solution)/shard_map/reduce_scatter | solution.py:101
  106.6 77.8 %copy-start.3 = (bf16[288,2048]{1,0:T(8,128)(2,1)S(1)}, bf16[288,2048]{1,0:T(8,128)(2,1)}, u32[]{:S(2)}) copy-start(bf16[288,2048]{1,0:T(8,128)(2,1)} %reshape.97) | copy-start | bytes 3538948
  110.9 78.4 %copy-start.2 = (bf16[288,2048]{1,0:T(8,128)(2,1)S(1)}, bf16[288,2048]{1,0:T(8,128)(2,1)}, u32[]{:S(2)}) copy-start(bf16[288,2048]{1,0:T(8,128)(2,1)} %reshape.101) | copy-start | bytes 3538948
  188.5 0.8 copy-start.10
  192.9 76.5 %copy-start.11 = (bf16[288,768]{1,0:T(8,128)(2,1)S(1)}, bf16[288,768]{1,0:T(8,128)(2,1)}, u32[]{:S(2)}) copy-start(bf16[288,768]{1,0:T(8,128)(2,1)} %copy-done.10) | copy-start | bytes 1327108
  273.7 45.3 %all-to-all-start.1 = ((bf16[16,18,2048]{2,1,0:T(8,128)(2,1)}), bf16[16,18,2048]{2,1,0:T(8,128)(2,1)S(1)}, u32[]{:S(2)}, u32[]{:S(2)}) async-start(bf16[16,18,2048]{2,1,0:T(8,128)(2,1)} %reshape.98), calls=%async_computation.1 | async-start | bytes 3145728 | tf_op jit(solution)/shard_map/all_to_all | solution.py:72
  281.2 3.5 copy-start.7
  281.2 3.5 copy-start.8
  284.8 1.9 copy-start.6
  284.8 2.1 copy-start.9
  319.1 42.8 %all-to-all-start.3 = ((bf16[16,18,2048]{2,1,0:T(8,128)(2,1)}), bf16[16,18,2048]{2,1,0:T(8,128)(2,1)}, u32[]{:S(2)}, u32[]{:S(2)}) async-start(bf16[16,18,2048]{2,1,0:T(8,128)(2,1)} %reshape.102), calls=%async_computation.3 | async-start | bytes 3145728 | tf_op jit(solution)/shard_map/all_to_all | solution.py:79
  326.2 37.2 %copy-start.4 = (bf16[288,2048,1]{1,0,2:T(8,128)(2,1)S(1)}, bf16[288,2048,1]{1,0,2:T(8,128)(2,1)}, u32[]{:S(2)}) copy-start(bf16[288,2048,1]{1,0,2:T(8,128)(2,1)} %reshape.107) | copy-start | bytes 3538948
Sparse Core Ops, SparseCore 0:
  11.1 88.1 all-gather.6
  102.5 81.7 all-gather.8
  187.6 81.7 all-gather.10
  274.3 224.7 reduce-scatter.1
where the time goes:
time: 506 us
  waiting for transfers between devices  413 us (82%)
  matrix products  28.8 us (6%)
  starting transfers between devices  27.9 us (6%)
  local copies, waits for them, and re-layouts  19.8 us (4%)
  between operations  14 us (3%)
    reduce_scatter x1, waiting for transfers between devices, shards(): lax.psum_scatter(lax.dot_general(part_hidden, dy_rows, (((0,), (0,)), (()...  131 us
    all_gather x1, waiting for transfers between devices, shards(): weight_rows = lax.all_gather(down_weight[0], 'dp', axis=0, tiled=True)  76.5 us
    all_gather x1, waiting for transfers between devices, shards(): lax.all_gather(up_weight[0], 'dp', axis=0, tiled=True)  73.5 us
    all_to_all x1, waiting for transfers between devices, shards(): lax.all_to_all(grad_rows.reshape(groups, capacity, features), 'expert', s...  35.6 us
    all_to_all x1, waiting for transfers between devices, shards(): lax.all_to_all(send_grad.reshape(groups, capacity, features), 'expert', s...  35.4 us
    all_to_all x1, waiting for transfers between devices, shards(): lax.all_to_all(send_rows.reshape(groups, capacity, features), 'expert', s...  30.6 us
    all_to_all x1, waiting for transfers between devices, shards(): lax.all_to_all(output.reshape(groups, capacity, features), 'expert', spli...  27.6 us
    all_to_all x1, starting transfers between devices, shards(): lax.all_to_all(send_rows.reshape(groups, capacity, features), 'expert', s...  10.6 us
  transfers between devices with their start and end apart: 8, of which 7 were waited for; matrix products, arithmetic and copies ran while one was open for 10% of the time, Pallas kernels for 0%

commit v1 on v0

--- a/solution.py
+++ b/solution.py
@@ -55,7 +55,9 @@
     active = gate_pre * sig_gate
     hidden = (active * up_pre).astype(jnp.bfloat16)
     contract = (((1,), (1,)), ((), ()))
-    weight_rows = lax.all_gather(down_weight[0], "dp", axis=0, tiled=True)
+    weight_rows = jnp.concatenate(
+        lax.all_to_all(jnp.stack([down_weight[0]] * lax.axis_size("dp")), "dp", 0, 0), axis=0
+    )
     part_hidden = hidden
     acc_part = jnp.dot(part_hidden, weight_rows, preferred_element_type=jnp.float32)
     back_part = lax.dot_general(dy_rows, weight_rows, contract, preferred_element_type=jnp.float32)

time: 506 us -> 449 us (0.89)
  waiting for transfers between devices: 413 us -> 346 us
  starting transfers between devices: 27.9 us -> 35.5 us
    all_gather x1 -> x0, waiting for transfers between devices: 76.5 us -> none  [shards(): weight_rows = lax.all_gather(down_weight[0], 'dp', axis=0, tiled=True)]
    all_gather x1, waiting for transfers between devices: 73.5 us -> 85.6 us  [shards(): lax.all_gather(up_weight[0], 'dp', axis=0, tiled=True)]
    all_to_all x0 -> x1, starting transfers between devices: none -> 10.1 us  [shards(): lax.all_to_all(jnp.stack([down_weight[0]] * lax.axis_size('dp')), 'dp', 0...]
  transfers between devices with their start and end apart: 8 -> 8, of which waited for: 7 -> 6; matrix products, arithmetic and copies ran while one was open for 10% -> 11% of each run, Pallas kernels for 0% -> 0%
where the time goes in v1:
time: 449 us; the launch traced here: 448 us
  waiting for transfers between devices  346 us (77%)
  starting transfers between devices  35.5 us (8%)
  matrix products  27.9 us (6%)
  local copies, waits for them, and re-layouts  22 us (5%)
  between operations  14 us (3%)
    reduce_scatter x1, waiting for transfers between devices, shards(): lax.psum_scatter(lax.dot_general(part_hidden, dy_rows, (((0,), (0,)), (()...  127 us
    all_gather x1, waiting for transfers between devices, shards(): lax.all_gather(up_weight[0], 'dp', axis=0, tiled=True)  85.6 us
    all_to_all x1, waiting for transfers between devices, shards(): lax.all_to_all(send_grad.reshape(groups, capacity, features), 'expert', s...  37.1 us
    all_to_all x1, waiting for transfers between devices, shards(): lax.all_to_all(grad_rows.reshape(groups, capacity, features), 'expert', s...  36.4 us
    all_to_all x1, waiting for transfers between devices, shards(): lax.all_to_all(send_rows.reshape(groups, capacity, features), 'expert', s...  30.6 us
    all_to_all x1, waiting for transfers between devices, shards(): lax.all_to_all(output.reshape(groups, capacity, features), 'expert', spli...  27.5 us
    all_to_all x1, starting transfers between devices, shards(): lax.all_to_all(send_rows.reshape(groups, capacity, features), 'expert', s...  10.6 us
    all_to_all x1, starting transfers between devices, shards(): lax.all_to_all(jnp.stack([down_weight[0]] * lax.axis_size('dp')), 'dp', 0...  10.1 us
  transfers between devices with their start and end apart: 8, of which 6 were waited for; matrix products, arithmetic and copies ran while one was open for 11% of the time, Pallas kernels for 0%

profile of v1, /device:TPU:16, one launch (start us, length us, event | category | flops | bytes accessed | tf_op | source)
XLA Modules:
  0.0 448.0 jit_solution(17510027363975098561)
XLA Ops:
  7.2 0.7 all-gather.5.cloned.1.call-update
  7.9 0.8 copy.29
  8.7 0.1 reshape.98
  8.8 0.1 eq.65
  9.0 0.6 reduce-window.6
  9.6 0.2 slice_reduce_fusion
  9.9 0.1 reduce_sum.42
  10.1 0.7 multiply_add_fusion.1
  10.9 0.5 convolution_convert_fusion.1
  11.3 1.4 reshape.100
  12.7 10.6 %all-to-all-start = ((bf16[16,18,2048]{2,1,0:T(8,128)(2,1)}), bf16[16,18,2048]{2,1,0:T(8,128)(2,1)}, u32[]{:S(2)}, u32[]{:S(2)}) async-start(bf16[16,18,2048]{2,1,0:T(8,128)(2,1)} %reshape.100), calls=%async_computation | async-start | bytes 3145728 | tf_op jit(solution)/shard_map/all_to_all | solution.py:31
  23.4 1.0 mul.83.clone
  24.4 2.4 mul.84
  27.0 0.1 mul.81
  27.1 2.1 convolution_convert_fusion.2
  29.3 1.4 reshape.105
  30.6 30.6 %all-to-all-done = bf16[16,18,2048]{2,1,0:T(8,128)(2,1)} async-done(((bf16[16,18,2048]{2,1,0:T(8,128)(2,1)}), bf16[16,18,2048]{2,1,0:T(8,128)(2,1)}, u32[]{:S(2)}, u32[]{:S(2)}) %all-to-all-start) | async-done | bytes 1179680 | tf_op jit(solution)/shard_map/all_to_all | solution.py:31
  61.3 4.8 %all-to-all-start.3 = ((bf16[16,18,2048]{2,1,0:T(8,128)(2,1)}), bf16[16,18,2048]{2,1,0:T(8,128)(2,1)S(1)}, u32[]{:S(2)}, u32[]{:S(2)}) async-start(bf16[16,18,2048]{2,1,0:T(8,128)(2,1)} %reshape.105), calls=%async_computation.3 | async-start | bytes 3145728 | tf_op jit(solution)/shard_map/all_to_all | solution.py:38
  66.1 0.7 all-gather.7.cloned.1.call-update
  66.8 37.1 %all-to-all-done.3 = bf16[16,18,2048]{2,1,0:T(8,128)(2,1)S(1)} async-done(((bf16[16,18,2048]{2,1,0:T(8,128)(2,1)}), bf16[16,18,2048]{2,1,0:T(8,128)(2,1)S(1)}, u32[]{:S(2)}, u32[]{:S(2)}) %all-to-all-start.3) | async-done | bytes 1179680 | tf_op jit(solution)/shard_map/all_to_all | solution.py:38
  103.9 2.0 stack.3
  105.9 10.1 %all-to-all-start.1 = ((bf16[32,24,2048]{2,1,0:T(8,128)(2,1)}), bf16[32,24,2048]{2,1,0:T(8,128)(2,1)}, u32[]{:S(2)}, u32[]{:S(2)}) async-start(bf16[32,24,2048]{2,1,0:T(8,128)(2,1)} %stack.3), calls=%async_computation.1 | async-start | bytes 6291456 | tf_op jit(solution)/shard_map/all_to_all | solution.py:59
  116.1 2.4 reshape.101
  118.5 1.2 reshape.106
  119.7 3.3 fusion.6
  123.1 85.6 %all-gather.7.cloned.1.call-done = bf16[1,2048,768]{2,1,0:T(8,128)(2,1)} async-done(((bf16[1,64,768]{2,1,0:T(8,128)(2,1)}), bf16[1,2048,768]{2,1,0:T(8,128)(2,1)}) %all-gather.7.cloned.1.call-update) | async-done | bytes 3145744 | tf_op jit(solution)/shard_map/all_gather | solution.py:50
  208.7 4.2 multiply_convert_fusion.4
  213.0 0.8 copy-done.10
  213.7 3.5 convolution_convert_fusion
  217.3 1.0 copy-done.11
  218.3 3.0 convolution_convert_fusion.3
  221.2 1.4 reshape.103
  222.6 5.1 %all-to-all-start.2 = ((bf16[16,18,2048]{2,1,0:T(8,128)(2,1)}), bf16[16,18,2048]{2,1,0:T(8,128)(2,1)S(1)}, u32[]{:S(2)}, u32[]{:S(2)}) async-start(bf16[16,18,2048]{2,1,0:T(8,128)(2,1)} %reshape.103), calls=%async_computation.2 | async-start | bytes 3145728 | tf_op jit(solution)/shard_map/all_to_all | solution.py:74
  227.7 3.6 fusion.31
  231.3 1.1 fusion
  232.5 0.7 copy-done.5
  233.2 0.2 copy-done.9
  233.4 2.2 fusion.11
  235.7 2.4 reshape.107
  238.1 27.5 %all-to-all-done.2 = bf16[16,18,2048]{2,1,0:T(8,128)(2,1)S(1)} async-done(((bf16[16,18,2048]{2,1,0:T(8,128)(2,1)}), bf16[16,18,2048]{2,1,0:T(8,128)(2,1)S(1)}, u32[]{:S(2)}, u32[]{:S(2)}) %all-to-all-start.2) | async-done | bytes 1179680 | tf_op jit(solution)/shard_map/all_to_all | solution.py:74
  265.6 4.8 %all-to-all-start.4 = ((bf16[16,18,2048]{2,1,0:T(8,128)(2,1)}), bf16[16,18,2048]{2,1,0:T(8,128)(2,1)}, u32[]{:S(2)}, u32[]{:S(2)}) async-start(bf16[16,18,2048]{2,1,0:T(8,128)(2,1)} %reshape.107), calls=%async_computation.4 | async-start | bytes 3145728 | tf_op jit(solution)/shard_map/all_to_all | solution.py:81
  270.4 1.1 convert_element_type.58
  271.5 0.4 reshape.111
  271.9 36.4 %all-to-all-done.4 = bf16[16,18,2048]{2,1,0:T(8,128)(2,1)} async-done(((bf16[16,18,2048]{2,1,0:T(8,128)(2,1)}), bf16[16,18,2048]{2,1,0:T(8,128)(2,1)}, u32[]{:S(2)}, u32[]{:S(2)}) %all-to-all-start.4) | async-done | bytes 1179680 | tf_op jit(solution)/shard_map/all_to_all | solution.py:81
  308.3 1.6 reshape.108
  309.9 3.0 multiply_reduce_fusion
  312.9 1.3 convolution_convert_fusion.4
  314.2 127.3 %reduce-scatter.2.cloned.1.call-done = bf16[24,2048]{1,0:T(8,128)(2,1)} async-done(((bf16[768,2048]{1,0:T(8,128)(2,1)}), bf16[24,2048]{1,0:T(8,128)(2,1)}) %reduce-scatter.2.cloned.1.call-update) | async-done | bytes 98320 | tf_op jit(solution)/shard_map/reduce_scatter | solution.py:103
  (34 shorter events, 0.5 us)
Async XLA Ops:
  7.2 3.7 copy-start
  7.2 112.6 %all-gather.5.cloned.1.call-start = ((), (), s32[]{:S(2)}) async-start(), calls=%async_computation.7 | async-start | bytes 3244032 | tf_op jit(solution)/shard_map/all_gather | solution.py:49
  12.7 10.6 %copy-start.1 = (bf16[128,2048]{1,0:T(8,128)(2,1)S(1)}, bf16[128,2048]{1,0:T(8,128)(2,1)}, u32[]{:S(2)}) copy-start(bf16[128,2048]{1,0:T(8,128)(2,1)} %param.8) | copy-start | bytes 1572868
  12.7 48.5 %all-to-all-start = ((bf16[16,18,2048]{2,1,0:T(8,128)(2,1)}), bf16[16,18,2048]{2,1,0:T(8,128)(2,1)}, u32[]{:S(2)}, u32[]{:S(2)}) async-start(bf16[16,18,2048]{2,1,0:T(8,128)(2,1)} %reshape.100), calls=%async_computation | async-start | bytes 3145728 | tf_op jit(solution)/shard_map/all_to_all | solution.py:31
  24.4 2.4 copy-start.4
  30.6 73.3 %copy-start.3 = (bf16[1,24,2048]{2,1,0:T(8,128)(2,1)S(1)}, bf16[1,24,2048]{2,1,0:T(8,128)(2,1)}, u32[]{:S(2)}) copy-start(bf16[1,24,2048]{2,1,0:T(8,128)(2,1)} %param.13) | copy-start | bytes 294916
  61.3 42.7 %all-to-all-start.3 = ((bf16[16,18,2048]{2,1,0:T(8,128)(2,1)}), bf16[16,18,2048]{2,1,0:T(8,128)(2,1)S(1)}, u32[]{:S(2)}, u32[]{:S(2)}) async-start(bf16[16,18,2048]{2,1,0:T(8,128)(2,1)} %reshape.105), calls=%async_computation.3 | async-start | bytes 3145728 | tf_op jit(solution)/shard_map/all_to_all | solution.py:38
  66.1 142.6 %all-gather.7.cloned.1.call-start = ((), (), s32[]{:S(2)}) async-start(), calls=%async_computation.8 | async-start | bytes 3244032 | tf_op jit(solution)/shard_map/all_gather | solution.py:50
  105.9 111.3 %all-to-all-start.1 = ((bf16[32,24,2048]{2,1,0:T(8,128)(2,1)}), bf16[32,24,2048]{2,1,0:T(8,128)(2,1)}, u32[]{:S(2)}, u32[]{:S(2)}) async-start(bf16[32,24,2048]{2,1,0:T(8,128)(2,1)} %stack.3), calls=%async_computation.1 | async-start | bytes 6291456 | tf_op jit(solution)/shard_map/all_to_all | solution.py:59
  116.1 325.4 %reduce-scatter.2.cloned.1.call-start = ((), (), s32[]{:S(2)}) async-start(), calls=%async_computation.6 | async-start | bytes 3244032 | tf_op jit(solution)/shard_map/reduce_scatter | solution.py:103
  123.1 89.9 %copy-start.7 = (f32[288,768]{1,0:T(8,128)}, f32[288,768]{1,0:T(8,128)S(1)}, u32[]{:S(2)}) copy-start(f32[288,768]{1,0:T(8,128)S(1)} %fusion.6) | copy-start | bytes 2654212
  123.1 90.6 %copy-start.2 = (bf16[288,2048]{1,0:T(8,128)(2,1)S(1)}, bf16[288,2048]{1,0:T(8,128)(2,1)}, u32[]{:S(2)}) copy-start(bf16[288,2048]{1,0:T(8,128)(2,1)} %reshape.106) | copy-start | bytes 3538948
  213.0 0.8 copy-start.10
  217.3 1.0 copy-start.11
  222.6 42.9 %all-to-all-start.2 = ((bf16[16,18,2048]{2,1,0:T(8,128)(2,1)}), bf16[16,18,2048]{2,1,0:T(8,128)(2,1)S(1)}, u32[]{:S(2)}, u32[]{:S(2)}) async-start(bf16[16,18,2048]{2,1,0:T(8,128)(2,1)} %reshape.103), calls=%async_computation.2 | async-start | bytes 3145728 | tf_op jit(solution)/shard_map/all_to_all | solution.py:74
  227.7 3.6 copy-start.6
  227.7 3.6 copy-start.8
  231.3 1.9 copy-start.5
  231.3 2.1 copy-start.9
  265.6 42.8 %all-to-all-start.4 = ((bf16[16,18,2048]{2,1,0:T(8,128)(2,1)}), bf16[16,18,2048]{2,1,0:T(8,128)(2,1)}, u32[]{:S(2)}, u32[]{:S(2)}) async-start(bf16[16,18,2048]{2,1,0:T(8,128)(2,1)} %reshape.107), calls=%async_computation.4 | async-start | bytes 3145728 | tf_op jit(solution)/shard_map/all_to_all | solution.py:81
Sparse Core Ops, SparseCore 0:
  11.1 88.1 all-gather.4
  102.5 106.1 all-gather.6
  217.4 224.0 reduce-scatter.1
